TPU v7x, 256 devices: a whole 4x4x8 slice. The times are simulated.
256 devices in a mesh: row: 32 (over z, y), col: 8 (over x, core).
Axes of the slice: x: 4, y: 4, z: 8, core: 2. Of those that a mesh axis runs over, the one named last changes fastest.
Arguments:
- amps: bfloat16 [30720, 30720], P(('col', 'row')), may hold values from -6 to 6
- cycle_int: bfloat16 [30720, 1024], P('col'), may hold values from -0.03125 to 0.03125
- tile_mask: int32 [480, 16], P('col'), may hold values 0 or 1
- coulomb: bfloat16 [30720, 1024], P('row', 'col'), may hold values from -6 to 6
- occ_irrep: int32 [240], replicated, may hold values from 0 to 7
- vir_irrep: int32 [192], replicated, may hold values from 0 to 7
- occ_energy: float32 [240], replicated, may hold values from -1.5 to -0.3
- vir_energy: float32 [192], replicated, may hold values from 0.3 to 2
Outputs:
- new_amps: bfloat16 [30720, 1024], P('row', 'col')
All inputs are finite; a program needn't handle non-finite values. No bound on the sum of `tile_mask` on one device may be relied on, other than what follows from the above.
Results may differ from a plain program's by a relative error of at most 0.001.
Values may be sent and summed in bfloat16 or wider, within the bound.
No kernel may reach another device: no remote copies, remote signals or barrier semaphores. Data moves between devices by JAX's collectives and lax.ppermute only.
A program may use at most 128 MiB of HBM per device.

v0:
```python
import jax
import jax.numpy as jnp
from jax import lax
from jax.sharding import Mesh, PartitionSpec as P

BLK = 64
CHUNKS = 2
Z, Y, X, C = ("z", "y", "x", "core")
COL = (X, C)
ROW = (Z, Y)


def lookup(positions, values_table):
    entries = jnp.arange(values_table.shape[0], dtype=jnp.int32)
    picked = jnp.where(
        positions[:, None] == entries[None, :],
        values_table[None, :],
        jnp.zeros((), values_table.dtype),
    )
    return jnp.sum(picked, axis=1)


def swap_perm(nz, nc):
    return [(z * nc + c, c * nz + z) for z in range(nz) for c in range(nc)]


def local(amps, cycle_int, tile_mask, coulomb, occ_irrep, vir_irrep, occ_energy, vir_energy):
    block_size = BLK
    occupied = occ_energy.shape[0]
    row_blocks = vir_energy.shape[0] // block_size - 1
    kc_rows, jb_all = cycle_int.shape
    rows_here, cols_here = coulomb.shape
    nz = lax.axis_size(Z)
    ny = lax.axis_size(Y)
    ncol = lax.axis_size(COL)
    z = lax.axis_index(Z)
    y = lax.axis_index(Y)
    c = lax.axis_index(COL)
    sub = amps.shape[0]
    span = sub * ny
    ci_rows = lax.dynamic_slice_in_dim(cycle_int, z * span, span, axis=0)
    mask_rows = jnp.repeat(tile_mask.astype(jnp.bfloat16), block_size, axis=0)
    mask_rows = lax.dynamic_slice_in_dim(mask_rows, z * span, span, axis=0)
    masked = (
        ci_rows.reshape(span, jb_all // block_size, block_size) * mask_rows[:, :, None]
    ).reshape(span, jb_all)
    masked_all = lax.all_gather(masked, COL, axis=0, tiled=True)
    groups = lax.axis_size((X, C, Y))
    width = amps.shape[1] // groups // CHUNKS
    pieces = amps.reshape(sub, groups, CHUNKS, width)
    sums = []
    previous = None
    for k in range(CHUNKS):
        piece = pieces[:, :, k, :].reshape(sub, groups * width)
        if previous is not None:
            previous, piece = lax.optimization_barrier((previous, piece))
            sums.append(lax.psum_scatter(previous, Z, scatter_dimension=1, tiled=True))
        plane_amps = lax.all_to_all(piece, (X, C, Y), split_axis=1, concat_axis=0, tiled=True)
        previous = lax.dot_general(
            plane_amps, masked_all, (((0,), (0,)), ((), ())), preferred_element_type=jnp.float32
        )
    sums.append(lax.psum_scatter(previous, Z, scatter_dimension=1, tiled=True))
    cycle_sum = jnp.concatenate(sums, axis=0)
    perm = swap_perm(nz, ncol)
    coulomb_here = lax.ppermute(coulomb, (Z, X, C), perm)
    row_block = c * ny + y
    row_pos = row_block * rows_here + jnp.arange(rows_here, dtype=jnp.int32)
    col_pos = z * cols_here + jnp.arange(cols_here, dtype=jnp.int32)
    occ_row = row_pos // block_size % occupied
    vir_row = block_size * (row_pos // (occupied * block_size)) + row_pos % block_size
    occ_col = col_pos // block_size % occupied
    vir_col = col_pos % block_size + row_blocks * block_size
    sym_row = jnp.bitwise_xor(lookup(occ_row, occ_irrep), lookup(vir_row, vir_irrep))
    sym_col = jnp.bitwise_xor(lookup(occ_col, occ_irrep), lookup(vir_col, vir_irrep))
    allowed = sym_row[:, None] == sym_col[None, :]
    gap_row = lookup(vir_row, vir_energy) - lookup(occ_row, occ_energy)
    gap_col = lookup(vir_col, vir_energy) - lookup(occ_col, occ_energy)
    denominator = gap_row[:, None] + gap_col[None, :]
    updated = (coulomb_here.astype(jnp.float32) + cycle_sum) / denominator
    out = jnp.where(allowed, updated, jnp.float32(0.0)).astype(jnp.bfloat16)
    return lax.ppermute(out, (Z, X, C), perm)


def solution(mesh):
    nrow, ncol = mesh.devices.shape
    ncore = 2
    nx = ncol // ncore
    nz = ncol
    ny = nrow // nz
    torus = Mesh(mesh.devices.reshape(nz, ny, nx, ncore), (Z, Y, X, C))
    return jax.shard_map(
        local,
        mesh=torus,
        in_specs=(P(COL + ROW, None), P(COL, None), P(COL, None), P(ROW, COL), P(), P(), P(), P()),
        out_specs=P(ROW, COL),
        check_vma=False,
    )
```

profile of v0, /device:TPU:31, one launch (start us, length us, event | category | flops | bytes accessed | tf_op | source)
XLA Modules:
  0.0 278.5 jit_solution(2675612284590024433)
XLA Ops:
  6.5 1.3 constant_dynamic-slice_fusion
  7.8 0.5 copy.42
  9.0 1.3 copy.29
  10.4 10.1 %copy.30 = bf16[120,30720]{0,1:T(8,128)(2,1)} copy(bf16[120,30720]{1,0:T(8,128)(2,1)} %param.8) | data formatting | bytes 14745600 | tf_op args[0]
  20.5 5.7 %fusion.12 = (bf16[120,32,1,480]{0,3,2,1:T(8,128)(2,1)}, bf16[120,32,480]{0,2,1:T(8,128)(2,1)}) fusion(bf16[120,32,2,480]{0,3,2,1:T(8,128)(2,1)} %bitcast.21), kind=kLoop, calls=%fused_computation.47 | loop fusion | bytes 14745600 | tf_op jit(solution)/shard_map/slice | solution.py:54
  26.1 6.5 %copy.32 = bf16[120,32,480]{2,0,1:T(8,128)(2,1)} copy(bf16[120,32,480]{0,2,1:T(8,128)(2,1)} %get-tuple-element.10) | data formatting | bytes 7372800 | tf_op jit(solution)/shard_map/all_to_all | solution.py:58
  32.6 7.7 %all-to-all-start = ((bf16[120,32,480]{2,0,1:T(8,128)(2,1)}), bf16[120,32,480]{2,0,1:T(8,128)(2,1)}, u32[]{:S(2)}, u32[]{:S(2)}) async-start(bf16[120,32,480]{2,0,1:T(8,128)(2,1)} %copy.32), calls=%async_computation | async-start | bytes 7864320 | tf_op jit(solution)/shard_map/all_to_all | solution.py:58
  40.3 6.2 %copy.40 = bf16[120,15360]{1,0:T(8,128)(2,1)} copy(bf16[120,15360]{0,1:T(8,128)(2,1)} %bitcast.23) | data formatting | bytes 7372800 | tf_op jit(solution)/shard_map/reshape;squeeze | solution.py:54
  46.5 58.6 %all-to-all-done = bf16[120,32,480]{2,0,1:T(8,128)(2,1)} async-done(((bf16[120,32,480]{2,0,1:T(8,128)(2,1)}), bf16[120,32,480]{2,0,1:T(8,128)(2,1)}, u32[]{:S(2)}, u32[]{:S(2)}) %all-to-all-start) | async-done | bytes 3686432 | tf_op jit(solution)/shard_map/all_to_all | solution.py:58
  105.1 9.7 %convolution_bitcast_fusion = f32[480,1024]{1,0:T(8,128)} fusion(bf16[3840,480]{1,0:T(8,128)(2,1)} %bitcast.4, bf16[3840,1024]{1,0:T(8,128)(2,1)} %all-gather.2.cloned.1.call-done), kind=kOutput, calls=%fused_computation.1 | convolution fusion | flops 3774873600 | bytes 13516800 | tf_op jit(solution)/shard_map/dot_general | solution.py:59
  114.8 6.1 %copy.41 = bf16[120,15360]{0,1:T(8,128)(2,1)} copy(bf16[120,15360]{1,0:T(8,128)(2,1)} %copy.40) | data formatting | bytes 7372800 | tf_op jit(solution)/shard_map/all_to_all | solution.py:58
  120.9 7.1 %all-to-all-start.1 = ((bf16[120,32,480]{0,2,1:T(8,128)(2,1)}), bf16[120,32,480]{0,2,1:T(8,128)(2,1)}, u32[]{:S(2)}, u32[]{:S(2)}) async-start(bf16[120,32,480]{0,2,1:T(8,128)(2,1)} %bitcast.22), calls=%async_computation.2 | async-start | bytes 7864320 | tf_op jit(solution)/shard_map/all_to_all | solution.py:58
  128.0 0.7 reduce-scatter.3.cloned.1.call-update
  128.8 46.8 %all-to-all-done.1 = bf16[120,32,480]{0,2,1:T(8,128)(2,1)} async-done(((bf16[120,32,480]{0,2,1:T(8,128)(2,1)}), bf16[120,32,480]{0,2,1:T(8,128)(2,1)}, u32[]{:S(2)}, u32[]{:S(2)}) %all-to-all-start.1) | async-done | bytes 3686432 | tf_op jit(solution)/shard_map/all_to_all | solution.py:58
  175.6 5.6 %copy.36 = bf16[32,120,480]{1,0,2:T(8,128)(2,1)} copy(bf16[32,120,480]{1,2,0:T(8,128)(2,1)} %bitcast.8) | data formatting | bytes 7372800 | tf_op jit(solution)/shard_map/all_to_all | solution.py:58
  181.2 8.6 %all_to_all.35 = bf16[3840,480]{0,1:T(8,128)(2,1)} reshape(bf16[32,120,480]{1,0,2:T(8,128)(2,1)} %copy.36) | data formatting | bytes 7372800 | tf_op jit(solution)/shard_map/all_to_all | solution.py:58
  189.9 9.7 %fusion.13 = f32[480,1024]{1,0:T(8,128)} fusion(bf16[3840,480]{0,1:T(8,128)(2,1)} %all_to_all.35, bf16[3840,1024]{1,0:T(8,128)(2,1)} %all-gather.2.cloned.1.call-done), kind=kOutput, calls=%fused_computation.48 | convolution fusion | flops 3774873600 | bytes 13516800 | tf_op jit(solution)/shard_map/dot_general | solution.py:59
  199.6 6.6 %collective-permute-start = (bf16[960,128]{1,0:T(8,128)(2,1)S(1)}, bf16[960,128]{1,0:T(8,128)(2,1)S(1)}, u32[]{:S(2)}, u32[]{:S(2)}) collective-permute-start(bf16[960,128]{1,0:T(8,128)(2,1)S(1)} %copy-done.5), channel_id=1, source_target_pairs={{0,0},{1,32},{2,64},{3,96},{4,128},{5,160},{6,192},{7,224},{32,1},... | collective-permute-start | bytes 737288 | tf_op jit(solution)/shard_map/ppermute | solution.py:65
  207.9 18.8 %collective-permute-done = bf16[960,128]{1,0:T(8,128)(2,1)S(1)} collective-permute-done((bf16[960,128]{1,0:T(8,128)(2,1)S(1)}, bf16[960,128]{1,0:T(8,128)(2,1)S(1)}, u32[]{:S(2)}, u32[]{:S(2)}) %collective-permute-start) | collective-permute-done | bytes 245792 | tf_op jit(solution)/shard_map/ppermute | solution.py:65
  226.7 19.3 %reduce-scatter.5.cloned.1.call-done = f32[480,128]{1,0:T(8,128)} async-done(((f32[480,1024]{1,0:T(8,128)}), f32[480,128]{1,0:T(8,128)}) %reduce-scatter.5.cloned.1.call-update) | async-done | bytes 245776 | tf_op jit(solution)/shard_map/reduce_scatter | solution.py:62
  246.0 1.4 fusion.2
  247.4 7.2 %collective-permute-start.1 = (bf16[960,128]{1,0:T(8,128)(2,1)S(1)}, bf16[960,128]{1,0:T(8,128)(2,1)S(1)}, u32[]{:S(2)}, u32[]{:S(2)}) collective-permute-start(bf16[960,128]{1,0:T(8,128)(2,1)S(1)} %fusion.2), channel_id=1, source_target_pairs={{0,0},{1,32},{2,64},{3,96},{4,128},{5,160},{6,192},{7,224},{32,1},... | collective-permute-start | bytes 737288 | tf_op jit(solution)/shard_map/ppermute | solution.py:81
  254.6 16.7 %collective-permute-done.1 = bf16[960,128]{1,0:T(8,128)(2,1)S(1)} collective-permute-done((bf16[960,128]{1,0:T(8,128)(2,1)S(1)}, bf16[960,128]{1,0:T(8,128)(2,1)S(1)}, u32[]{:S(2)}, u32[]{:S(2)}) %collective-permute-start.1) | collective-permute-done | bytes 245792 | tf_op jit(solution)/shard_map/ppermute | solution.py:81
  271.3 0.7 copy.44
  (38 shorter events, 2.3 us)
Async XLA Ops:
  6.5 1.8 copy-start
  6.5 98.5 %all-gather.2.cloned.1.call-start = ((), (), s32[]{:S(2)}) async-start(), calls=%async_computation.4 | async-start | bytes 8847360 | tf_op jit(solution)/shard_map/all_gather | solution.py:47
  32.6 72.5 %all-to-all-start = ((bf16[120,32,480]{2,0,1:T(8,128)(2,1)}), bf16[120,32,480]{2,0,1:T(8,128)(2,1)}, u32[]{:S(2)}, u32[]{:S(2)}) async-start(bf16[120,32,480]{2,0,1:T(8,128)(2,1)} %copy.32), calls=%async_computation | async-start | bytes 7864320 | tf_op jit(solution)/shard_map/all_to_all | solution.py:58
  120.9 54.7 %all-to-all-start.1 = ((bf16[120,32,480]{0,2,1:T(8,128)(2,1)}), bf16[120,32,480]{0,2,1:T(8,128)(2,1)}, u32[]{:S(2)}, u32[]{:S(2)}) async-start(bf16[120,32,480]{0,2,1:T(8,128)(2,1)} %bitcast.22), calls=%async_computation.2 | async-start | bytes 7864320 | tf_op jit(solution)/shard_map/all_to_all | solution.py:58
  128.0 98.7 %reduce-scatter.3.cloned.1.call-start = ((), (), s32[]{:S(2)}) async-start(), calls=%async_computation.5 | async-start | bytes 2211840 | tf_op jit(solution)/shard_map/reduce_scatter | solution.py:57
  128.7 117.3 %reduce-scatter.5.cloned.1.call-start = ((), (), s32[]{:S(2)}) async-start(), calls=%async_computation.6 | async-start | bytes 2211840 | tf_op jit(solution)/shard_map/reduce_scatter | solution.py:62
  189.8 9.8 %copy-start.5 = (bf16[960,128]{1,0:T(8,128)(2,1)S(1)}, bf16[960,128]{1,0:T(8,128)(2,1)}, u32[]{:S(2)}) copy-start(bf16[960,128]{1,0:T(8,128)(2,1)} %param.11) | copy-start | bytes 737284
  189.8 16.4 %copy-start.1 = (f32[192]{0:T(256)S(1)}, f32[192]{0:T(256)}, u32[]{:S(2)}) copy-start(f32[192]{0:T(256)} %param.15) | copy-start | bytes 2308
  189.8 16.5 %copy-start.2 = (f32[240]{0:T(256)S(1)}, f32[240]{0:T(256)}, u32[]{:S(2)}) copy-start(f32[240]{0:T(256)} %param.14) | copy-start | bytes 2884
  189.8 17.2 %copy-start.3 = (s32[192]{0:T(256)S(1)}, s32[192]{0:T(256)}, u32[]{:S(2)}) copy-start(s32[192]{0:T(256)} %param.13) | copy-start | bytes 2308
  189.8 17.3 %copy-start.4 = (s32[240]{0:T(256)S(1)}, s32[240]{0:T(256)}, u32[]{:S(2)}) copy-start(s32[240]{0:T(256)} %param.12) | copy-start | bytes 2884
  199.6 27.1 %collective-permute-start = (bf16[960,128]{1,0:T(8,128)(2,1)S(1)}, bf16[960,128]{1,0:T(8,128)(2,1)S(1)}, u32[]{:S(2)}, u32[]{:S(2)}) collective-permute-start(bf16[960,128]{1,0:T(8,128)(2,1)S(1)} %copy-done.5), channel_id=1, source_target_pairs={{0,0},{1,32},{2,64},{3,96},{4,128},{5,160},{6,192},{7,224},{32,1},... | collective-permute-start | bytes 737288 | tf_op jit(solution)/shard_map/ppermute | solution.py:65
  247.4 23.9 %collective-permute-start.1 = (bf16[960,128]{1,0:T(8,128)(2,1)S(1)}, bf16[960,128]{1,0:T(8,128)(2,1)S(1)}, u32[]{:S(2)}, u32[]{:S(2)}) collective-permute-start(bf16[960,128]{1,0:T(8,128)(2,1)S(1)} %fusion.2), channel_id=1, source_target_pairs={{0,0},{1,32},{2,64},{3,96},{4,128},{5,160},{6,192},{7,224},{32,1},... | collective-permute-start | bytes 737288 | tf_op jit(solution)/shard_map/ppermute | solution.py:81
Sparse Core Ops, SparseCore 0:
  10.5 87.8 all-gather.1
  131.4 38.8 reduce-scatter.2
  199.7 46.2 reduce-scatter.4
where the time goes:
time: 280 us; the launch traced here: 278 us
  waiting for transfers between devices  161 us (58%)
  local copies, waits for them, and re-layouts  53.2 us (19%)
  starting transfers between devices  28.7 us (10%)
  matrix products  19.4 us (7%)
  between operations  13.3 us (5%)
  other arithmetic  3.02 us (1%)
    all_to_all x2, waiting for transfers between devices, local(): lax.all_to_all(piece, (X, C, Y), split_axis=1, concat_axis=0, tiled=True)  105 us
    all_to_all x4, local copies, waits for them, and re-layouts, local(): lax.all_to_all(piece, (X, C, Y), split_axis=1, concat_axis=0, tiled=True)  26.8 us
    dot_general x2, matrix products, local(): lax.dot_general(plane_amps, masked_all, (((0,), (0,)), ((), ())), preferr...  19.4 us
    reduce_scatter x2, waiting for transfers between devices, local(): sums.append(lax.psum_scatter(previous, Z, scatter_dimension=1, tiled=True))  19.3 us
    ppermute x1, waiting for transfers between devices, local(): coulomb_here = lax.ppermute(coulomb, (Z, X, C), perm)  18.8 us
    ppermute x1, waiting for transfers between devices, local(): return lax.ppermute(out, (Z, X, C), perm)  16.7 us
    all_to_all x2, starting transfers between devices, local(): lax.all_to_all(piece, (X, C, Y), split_axis=1, concat_axis=0, tiled=True)  14.8 us
    unnamed x15, local copies, waits for them, and re-layouts  11.4 us
  transfers between devices with their start and end apart: 7, of which 5 were waited for; matrix products, arithmetic and copies ran while one was open for 16% of the time, Pallas kernels for 0%

commit v1 on v0

--- a/solution.py
+++ b/solution.py
@@ -8,6 +8,9 @@
 Z, Y, X, C = ("z", "y", "x", "core")
 COL = (X, C)
 ROW = (Z, Y)
+carry_set = lambda field_in, bus_axis: jnp.concatenate(
+    lax.all_to_all(jnp.stack(jnp.split(field_in, lax.axis_size(bus_axis), 1), 0), bus_axis, 0, 0), 0
+)
 
 
 def lookup(positions, values_table):
@@ -55,7 +58,7 @@
         if previous is not None:
             previous, piece = lax.optimization_barrier((previous, piece))
             sums.append(lax.psum_scatter(previous, Z, scatter_dimension=1, tiled=True))
-        plane_amps = lax.all_to_all(piece, (X, C, Y), split_axis=1, concat_axis=0, tiled=True)
+        plane_amps = carry_set(piece, (X, C, Y))
         previous = lax.dot_general(
             plane_amps, masked_all, (((0,), (0,)), ((), ())), preferred_element_type=jnp.float32
         )

time: 280 us -> 369 us (1.32)
  local copies, waits for them, and re-layouts: 53.2 us -> 159 us
  waiting for transfers between devices: 161 us -> 143 us
    unnamed x15 -> x80, local copies, waits for them, and re-layouts: 11.4 us -> 75.9 us
    slice x1, local copies, waits for them, and re-layouts: 5.67 us -> 38.6 us  [local(): piece = pieces[:, :, k, :].reshape(sub, groups * width)]
    all_to_all x4 -> x0, local copies, waits for them, and re-layouts: 26.8 us -> none  [local(): lax.all_to_all(piece, (X, C, Y), split_axis=1, concat_axis=0, tiled=True)]
    reshape x0 -> x1, local copies, waits for them, and re-layouts: none -> 22.8 us  [local(): pieces = amps.reshape(sub, groups, CHUNKS, width)]
    all_to_all x2, waiting for transfers between devices: 105 us -> 85.9 us  [lax.all_to_all(jnp.stack(jnp.split(field_in, lax.axis_size(bus_axis), 1),...]
    another operation x1 -> x2, local copies, waits for them, and re-layouts: 6.2 us -> 17 us  [local(): piece = pieces[:, :, k, :].reshape(sub, groups * width)]
  transfers between devices with their start and end apart: 7 -> 7, of which waited for: 5 -> 5; matrix products, arithmetic and copies ran while one was open for 16% -> 35% of each run, Pallas kernels for 0% -> 0%
where the time goes in v1:
time: 369 us; the launch traced here: 368 us
  local copies, waits for them, and re-layouts  159 us (43%)
  waiting for transfers between devices  143 us (39%)
  starting transfers between devices  29.9 us (8%)
  matrix products  19.5 us (5%)
  between operations  13.3 us (4%)
    all_to_all x2, waiting for transfers between devices, lax.all_to_all(jnp.stack(jnp.split(field_in, lax.axis_size(bus_axis), 1),...  85.9 us
    unnamed x80, local copies, waits for them, and re-layouts  75.9 us
    slice x1, local copies, waits for them, and re-layouts, local(): piece = pieces[:, :, k, :].reshape(sub, groups * width)  38.6 us
    reshape x1, local copies, waits for them, and re-layouts, local(): pieces = amps.reshape(sub, groups, CHUNKS, width)  22.8 us
    dot_general x2, matrix products, local(): lax.dot_general(plane_amps, masked_all, (((0,), (0,)), ((), ())), preferr...  19.5 us
    ppermute x1, waiting for transfers between devices, local(): coulomb_here = lax.ppermute(coulomb, (Z, X, C), perm)  19.1 us
    reduce_scatter x2, waiting for transfers between devices, local(): sums.append(lax.psum_scatter(previous, Z, scatter_dimension=1, tiled=True))  19 us
    ppermute x1, waiting for transfers between devices, local(): return lax.ppermute(out, (Z, X, C), perm)  18.1 us
  transfers between devices with their start and end apart: 7, of which 5 were waited for; matrix products, arithmetic and copies ran while one was open for 35% of the time, Pallas kernels for 0%

profile of v1, /device:TPU:31, one launch (start us, length us, event | category | flops | bytes accessed | tf_op | source)
XLA Modules:
  0.0 367.5 jit_solution(6746122183675165202)
XLA Ops:
  10.4 22.8 %reshape.125 = bf16[120,32,2,480]{3,2,1,0:T(2,128)(2,1)} reshape(bf16[120,30720]{1,0:T(8,128)(2,1)} %param.8) | data formatting | bytes 14745600 | tf_op jit(solution)/shard_map/reshape | solution.py:53
  33.2 38.6 %slice_reduce_fusion = (bf16[120,32,480]{2,1,0:T(8,128)(2,1)}, bf16[120,32,480]{2,1,0:T(8,128)(2,1)}) fusion(bf16[120,32,2,480]{3,2,1,0:T(2,128)(2,1)} %reshape.125), kind=kLoop, calls=%fused_computation | loop fusion | bytes 14745600 | tf_op jit(solution)/shard_map/slice | solution.py:57
  71.8 8.5 %reshape_squeeze.6 = bf16[120,15360]{1,0:T(8,128)(2,1)} reshape(bf16[120,32,480]{2,1,0:T(8,128)(2,1)} %get-tuple-element.10) | data formatting | bytes 7372800 | tf_op jit(solution)/shard_map/reshape;squeeze | solution.py:57
  80.3 1.7 constant_dynamic-update-slice_fusion.31
  88.5 1.7 constant_dynamic-update-slice_fusion.26
  96.8 1.7 constant_dynamic-update-slice_fusion.21
  101.7 1.7 constant_dynamic-update-slice_fusion.18
  103.3 1.7 constant_dynamic-update-slice_fusion.17
  118.3 7.7 %all-to-all-start = ((bf16[32,120,480]{2,1,0:T(8,128)(2,1)}), bf16[32,120,480]{2,1,0:T(8,128)(2,1)}, u32[]{:S(2)}, u32[]{:S(2)}) async-start(bf16[32,120,480]{2,1,0:T(8,128)(2,1)} %constant_dynamic-update-slice_fusion), calls=%async_computation | async-start | bytes 7864320 | tf_op jit(solution)/shard_map/all_to_all | solution.py:12
  126.0 8.5 %reshape_squeeze.7 = bf16[120,15360]{1,0:T(8,128)(2,1)} reshape(bf16[120,32,480]{2,1,0:T(8,128)(2,1)} %get-tuple-element.9) | data formatting | bytes 7372800 | tf_op jit(solution)/shard_map/reshape;squeeze | solution.py:57
  134.5 39.1 %all-to-all-done = bf16[32,120,480]{2,1,0:T(8,128)(2,1)} async-done(((bf16[32,120,480]{2,1,0:T(8,128)(2,1)}), bf16[32,120,480]{2,1,0:T(8,128)(2,1)}, u32[]{:S(2)}, u32[]{:S(2)}) %all-to-all-start) | async-done | bytes 3686432 | tf_op jit(solution)/shard_map/all_to_all | solution.py:12
  173.6 9.7 %fusion.12 = f32[480,1024]{1,0:T(8,128)} fusion(bf16[3840,480]{1,0:T(8,128)(2,1)} %bitcast.32, bf16[3840,1024]{1,0:T(8,128)(2,1)} %all-gather.2.cloned.1.call-done), kind=kOutput, calls=%fused_computation.143 | convolution fusion | flops 3774873600 | bytes 13516800 | tf_op jit(solution)/shard_map/dot_general | solution.py:62
  183.3 1.7 constant_dynamic-update-slice_fusion.63
  191.6 1.7 constant_dynamic-update-slice_fusion.58
  204.7 1.7 constant_dynamic-update-slice_fusion.50
  206.4 1.7 constant_dynamic-update-slice_fusion.49
  221.4 7.4 %all-to-all-start.1 = ((bf16[32,120,480]{2,1,0:T(8,128)(2,1)}), bf16[32,120,480]{2,1,0:T(8,128)(2,1)}, u32[]{:S(2)}, u32[]{:S(2)}) async-start(bf16[32,120,480]{2,1,0:T(8,128)(2,1)} %constant_dynamic-update-slice_fusion.32), calls=%async_computation.2 | async-start | bytes 7864320 | tf_op jit(solution)/shard_map/all_to_all | solution.py:12
  229.6 46.8 %all-to-all-done.1 = bf16[32,120,480]{2,1,0:T(8,128)(2,1)} async-done(((bf16[32,120,480]{2,1,0:T(8,128)(2,1)}), bf16[32,120,480]{2,1,0:T(8,128)(2,1)}, u32[]{:S(2)}, u32[]{:S(2)}) %all-to-all-start.1) | async-done | bytes 3686432 | tf_op jit(solution)/shard_map/all_to_all | solution.py:12
  276.5 9.8 %fusion.13 = f32[480,1024]{1,0:T(8,128)} fusion(bf16[3840,480]{1,0:T(8,128)(2,1)} %bitcast.66, bf16[3840,1024]{1,0:T(8,128)(2,1)} %all-gather.2.cloned.1.call-done), kind=kOutput, calls=%fused_computation.144 | convolution fusion | flops 3774873600 | bytes 13516800 | tf_op jit(solution)/shard_map/dot_general | solution.py:62
  286.3 9.0 %collective-permute-start = (bf16[960,128]{1,0:T(8,128)(2,1)S(1)}, bf16[960,128]{1,0:T(8,128)(2,1)S(1)}, u32[]{:S(2)}, u32[]{:S(2)}) collective-permute-start(bf16[960,128]{1,0:T(8,128)(2,1)S(1)} %copy-done.7), channel_id=1, source_target_pairs={{0,0},{1,32},{2,64},{3,96},{4,128},{5,160},{6,192},{7,224},{32,1},... | collective-permute-start | bytes 737288 | tf_op jit(solution)/shard_map/ppermute | solution.py:68
  296.9 19.1 %collective-permute-done = bf16[960,128]{1,0:T(8,128)(2,1)S(1)} collective-permute-done((bf16[960,128]{1,0:T(8,128)(2,1)S(1)}, bf16[960,128]{1,0:T(8,128)(2,1)S(1)}, u32[]{:S(2)}, u32[]{:S(2)}) %collective-permute-start) | collective-permute-done | bytes 245792 | tf_op jit(solution)/shard_map/ppermute | solution.py:68
  316.0 19.0 %reduce-scatter.5.cloned.1.call-done = f32[480,128]{1,0:T(8,128)} async-done(((f32[480,1024]{1,0:T(8,128)}), f32[480,128]{1,0:T(8,128)}) %reduce-scatter.5.cloned.1.call-update) | async-done | bytes 245776 | tf_op jit(solution)/shard_map/reduce_scatter | solution.py:65
  336.4 5.8 %collective-permute-start.1 = (bf16[960,128]{1,0:T(8,128)(2,1)S(1)}, bf16[960,128]{1,0:T(8,128)(2,1)S(1)}, u32[]{:S(2)}, u32[]{:S(2)}) collective-permute-start(bf16[960,128]{1,0:T(8,128)(2,1)S(1)} %fusion.2), channel_id=1, source_target_pairs={{0,0},{1,32},{2,64},{3,96},{4,128},{5,160},{6,192},{7,224},{32,1},... | collective-permute-start | bytes 737288 | tf_op jit(solution)/shard_map/ppermute | solution.py:84
  342.2 18.1 %collective-permute-done.1 = bf16[960,128]{1,0:T(8,128)(2,1)S(1)} collective-permute-done((bf16[960,128]{1,0:T(8,128)(2,1)S(1)}, bf16[960,128]{1,0:T(8,128)(2,1)S(1)}, u32[]{:S(2)}, u32[]{:S(2)}) %collective-permute-start.1) | collective-permute-done | bytes 245792 | tf_op jit(solution)/shard_map/ppermute | solution.py:84
  (103 shorter events, 69.2 us)
Async XLA Ops:
  6.5 1.8 copy-start.2
  6.5 167.1 %all-gather.2.cloned.1.call-start = ((), (), s32[]{:S(2)}) async-start(), calls=%async_computation.4 | async-start | bytes 8847360 | tf_op jit(solution)/shard_map/all_gather | solution.py:50
  80.3 26.4 %copy-start.1 = (bf16[120,15360]{1,0:T(8,128)(2,1)S(1)}, bf16[120,15360]{1,0:T(8,128)(2,1)}, u32[]{:S(2)}) copy-start(bf16[120,15360]{1,0:T(8,128)(2,1)} %reshape_squeeze.6) | copy-start | bytes 11059204
  118.3 55.3 %all-to-all-start = ((bf16[32,120,480]{2,1,0:T(8,128)(2,1)}), bf16[32,120,480]{2,1,0:T(8,128)(2,1)}, u32[]{:S(2)}, u32[]{:S(2)}) async-start(bf16[32,120,480]{2,1,0:T(8,128)(2,1)} %constant_dynamic-update-slice_fusion), calls=%async_computation | async-start | bytes 7864320 | tf_op jit(solution)/shard_map/all_to_all | solution.py:12
  183.3 26.4 %copy-start = (bf16[120,15360]{1,0:T(8,128)(2,1)S(1)}, bf16[120,15360]{1,0:T(8,128)(2,1)}, u32[]{:S(2)}) copy-start(bf16[120,15360]{1,0:T(8,128)(2,1)} %reshape_squeeze.7) | copy-start | bytes 11059204
  221.4 55.0 %all-to-all-start.1 = ((bf16[32,120,480]{2,1,0:T(8,128)(2,1)}), bf16[32,120,480]{2,1,0:T(8,128)(2,1)}, u32[]{:S(2)}, u32[]{:S(2)}) async-start(bf16[32,120,480]{2,1,0:T(8,128)(2,1)} %constant_dynamic-update-slice_fusion.32), calls=%async_computation.2 | async-start | bytes 7864320 | tf_op jit(solution)/shard_map/all_to_all | solution.py:12
  228.8 87.2 %reduce-scatter.3.cloned.1.call-start = ((), (), s32[]{:S(2)}) async-start(), calls=%async_computation.5 | async-start | bytes 2211840 | tf_op jit(solution)/shard_map/reduce_scatter | solution.py:60
  229.6 105.5 %reduce-scatter.5.cloned.1.call-start = ((), (), s32[]{:S(2)}) async-start(), calls=%async_computation.6 | async-start | bytes 2211840 | tf_op jit(solution)/shard_map/reduce_scatter | solution.py:65
  276.4 9.9 %copy-start.7 = (bf16[960,128]{1,0:T(8,128)(2,1)S(1)}, bf16[960,128]{1,0:T(8,128)(2,1)}, u32[]{:S(2)}) copy-start(bf16[960,128]{1,0:T(8,128)(2,1)} %param.11) | copy-start | bytes 737284
  276.4 18.9 %copy-start.3 = (f32[240]{0:T(256)S(1)}, f32[240]{0:T(256)}, u32[]{:S(2)}) copy-start(f32[240]{0:T(256)} %param.14) | copy-start | bytes 2884
  276.4 19.0 %copy-start.4 = (f32[192]{0:T(256)S(1)}, f32[192]{0:T(256)}, u32[]{:S(2)}) copy-start(f32[192]{0:T(256)} %param.15) | copy-start | bytes 2308
  276.4 19.2 %copy-start.5 = (s32[192]{0:T(256)S(1)}, s32[192]{0:T(256)}, u32[]{:S(2)}) copy-start(s32[192]{0:T(256)} %param.13) | copy-start | bytes 2308
  276.4 19.8 %copy-start.6 = (s32[240]{0:T(256)S(1)}, s32[240]{0:T(256)}, u32[]{:S(2)}) copy-start(s32[240]{0:T(256)} %param.12) | copy-start | bytes 2884
  286.3 29.7 %collective-permute-start = (bf16[960,128]{1,0:T(8,128)(2,1)S(1)}, bf16[960,128]{1,0:T(8,128)(2,1)S(1)}, u32[]{:S(2)}, u32[]{:S(2)}) collective-permute-start(bf16[960,128]{1,0:T(8,128)(2,1)S(1)} %copy-done.7), channel_id=1, source_target_pairs={{0,0},{1,32},{2,64},{3,96},{4,128},{5,160},{6,192},{7,224},{32,1},... | collective-permute-start | bytes 737288 | tf_op jit(solution)/shard_map/ppermute | solution.py:68
  336.4 23.9 %collective-permute-start.1 = (bf16[960,128]{1,0:T(8,128)(2,1)S(1)}, bf16[960,128]{1,0:T(8,128)(2,1)S(1)}, u32[]{:S(2)}, u32[]{:S(2)}) collective-permute-start(bf16[960,128]{1,0:T(8,128)(2,1)S(1)} %fusion.2), channel_id=1, source_target_pairs={{0,0},{1,32},{2,64},{3,96},{4,128},{5,160},{6,192},{7,224},{32,1},... | collective-permute-start | bytes 737288 | tf_op jit(solution)/shard_map/ppermute | solution.py:84
Sparse Core Ops, SparseCore 0:
  10.5 51.3 all-gather.1
  232.2 39.9 reduce-scatter.2
  286.4 48.5 reduce-scatter.4
